TPU v7x, 512 devices: a whole 4x8x8 slice. The times are simulated.
512 devices in a mesh: heads: 8 (over y), ctx: 64 (over z, x, core).
Axes of the slice: x: 4, y: 8, z: 8, core: 2. Of those that a mesh axis runs over, the one named last changes fastest.
Arguments:
- queries: bfloat16 [16384, 4096], P('ctx', 'heads'), may hold values from -6 to 6
- keys: bfloat16 [16384, 1024], P('ctx', 'heads'), may hold values from -6 to 6
- values: bfloat16 [16384, 1024], P('ctx', 'heads'), may hold values from -6 to 6
- out_weight: bfloat16 [4096, 4096], P('heads'), may hold values from -0.09375 to 0.09375
- out_grad: bfloat16 [4096, 16384], P('heads', 'ctx'), may hold values from -6 to 6
- doc_lengths: int32 [16], replicated, may hold values from 1 to 1792, 16384 in all
Outputs:
- out_t: bfloat16 [4096, 16384], P('heads', 'ctx')
- grad_q: bfloat16 [16384, 4096], P('ctx', 'heads')
- grad_k: bfloat16 [16384, 1024], P('ctx', 'heads')
- grad_v: bfloat16 [16384, 1024], P('ctx', 'heads')
Inputs may be any that keep to these rules, and one draw needn't show every extreme that they name: `doc_lengths`: the 16 lengths sum to 16384; the longest document has exactly 1792 tokens.
All inputs are finite; a program needn't handle non-finite values.
Results may differ from a plain program's by a relative error of at most 0.02.
Values may be sent and summed in bfloat16 or wider, within the bound.
No kernel may reach another device: no remote copies, remote signals or barrier semaphores. Data moves between devices by JAX's collectives and lax.ppermute only.
A program may use at most 64 MiB of HBM per device.

v0:
```python
import math
import jax
import jax.numpy as jnp
from jax import lax
from jax.sharding import PartitionSpec as P

REACH = 7


def passed_along(value, axis, steps):
    count = lax.axis_size(axis)
    first, last = (max(0, -steps), min(count, count - steps))
    return lax.ppermute(value, axis, [(source, source + steps) for source in range(first, last)])


def per_device(queries, keys, values, out_weight, out_grad, doc_lengths):
    tok_rows = queries.shape[0]
    head_dim = keys.shape[1]
    group_size = queries.shape[1] // head_dim
    scaling = 1.0 / math.sqrt(head_dim)
    shard = lax.axis_index("ctx")
    doc_ends = jnp.cumsum(doc_lengths)
    starts = doc_ends - doc_lengths
    positions = shard * tok_rows + jnp.arange(tok_rows, dtype=jnp.int32)
    first_key = jnp.max(
        jnp.where(starts[None, :] <= positions[:, None], starts[None, :], 0), axis=1
    )
    stacked = jnp.concatenate([keys, values], axis=1)
    blocks = [stacked[None]]
    for offset in range(1, REACH + 1):
        blocks.append(passed_along(stacked, "ctx", offset)[None])
    window = jnp.concatenate(blocks, axis=0)
    num_blocks = window.shape[0]
    flat_keys = window[:, :, :head_dim].reshape(num_blocks * tok_rows, head_dim)
    flat_values = window[:, :, head_dim:].reshape(num_blocks * tok_rows, head_dim)
    key_pos = (
        (shard - jnp.arange(num_blocks, dtype=jnp.int32))[:, None] * tok_rows
        + jnp.arange(tok_rows, dtype=jnp.int32)[None, :]
    ).reshape(-1)
    visible = (key_pos[None, :] >= first_key[:, None]) & (key_pos[None, :] <= positions[:, None])
    query_heads = queries.reshape(tok_rows, group_size, head_dim)
    scores = (
        jnp.einsum("tgd,kd->gtk", query_heads, flat_keys, preferred_element_type=jnp.float32)
        * scaling
    )
    scores = jnp.where(visible[None], scores, -jnp.inf)
    largest = jnp.max(scores, axis=-1, keepdims=True)
    expons = jnp.exp(scores - largest)
    weights = expons / jnp.sum(expons, axis=-1, keepdims=True)
    probs = weights.astype(jnp.bfloat16)
    attn_heads = jnp.einsum(
        "gtk,kd->tgd", probs, flat_values, preferred_element_type=jnp.float32
    ).astype(jnp.bfloat16)
    attn = attn_heads.reshape(tok_rows, group_size * head_dim)
    columns = out_weight
    out_t = lax.psum_scatter(
        lax.dot_general(
            columns, attn, (((0,), (1,)), ((), ())), preferred_element_type=jnp.float32
        ),
        "heads",
        scatter_dimension=0,
        tiled=True,
    ).astype(jnp.bfloat16)
    columns = out_weight
    grad_attn = jnp.dot(
        columns,
        lax.all_gather(out_grad, "heads", axis=0, tiled=True),
        preferred_element_type=jnp.float32,
    ).astype(jnp.bfloat16)
    grad_heads = grad_attn.reshape(group_size, head_dim, tok_rows)
    delta_sum = jnp.einsum(
        "tgd,gdt->gt", attn_heads, grad_heads, preferred_element_type=jnp.float32
    )
    grad_probs = jnp.einsum(
        "gdt,kd->gtk", grad_heads, flat_values, preferred_element_type=jnp.float32
    )
    dscore = (weights * (grad_probs - delta_sum[:, :, None]) * scaling).astype(jnp.bfloat16)
    grad_q = (
        jnp.einsum("gtk,kd->tgd", dscore, flat_keys, preferred_element_type=jnp.float32)
        .astype(jnp.bfloat16)
        .reshape(tok_rows, group_size * head_dim)
    )
    key_part = jnp.einsum("gtk,tgd->kd", dscore, query_heads, preferred_element_type=jnp.float32)
    value_part = jnp.einsum("gtk,gdt->kd", probs, grad_heads, preferred_element_type=jnp.float32)
    partial_grads = jnp.concatenate([key_part, value_part], axis=1).reshape(
        num_blocks, tok_rows, 2 * head_dim
    )
    summed = partial_grads[0]
    for offset in range(1, num_blocks):
        summed = summed + passed_along(partial_grads[offset], "ctx", -offset)
    grad_k = summed[:, :head_dim].astype(jnp.bfloat16)
    grad_v = summed[:, head_dim:].astype(jnp.bfloat16)
    return (out_t, grad_q, grad_k, grad_v)


def solution(mesh):
    placed = (
        P("ctx", "heads"),
        P("ctx", "heads"),
        P("ctx", "heads"),
        P("heads", None),
        P("heads", "ctx"),
        P(),
    )
    return jax.shard_map(
        per_device,
        mesh=mesh,
        in_specs=placed,
        out_specs=(P("heads", "ctx"), P("ctx", "heads"), P("ctx", "heads"), P("ctx", "heads")),
        check_vma=False,
    )
```

profile of v0, /device:TPU:10, one launch (start us, length us, event | category | flops | bytes accessed | tf_op | source)
XLA Modules:
  0.0 153.6 jit_solution(13572130763276567545)
XLA Ops:
  7.2 0.0 all-gather.2.cloned.1.call-start
  7.2 0.9 constant_dynamic-update-slice_fusion.1
  8.1 0.9 constant_dynamic-update-slice_fusion
  8.9 3.7 %collective-permute-start.6 = (bf16[256,256]{1,0:T(8,128)(2,1)S(1)}, bf16[256,256]{1,0:T(8,128)(2,1)S(1)}, u32[]{:S(2)}, u32[]{:S(2)}) collective-permute-start(bf16[256,256]{1,0:T(8,128)(2,1)S(1)} %constant_dynamic-update-slice_fusion), channel_id=1, source_target_pairs={{0,7},{1,8},{2,9},{3,10},{4,11},{5,12},{6,13},{7,14},{8,15},{9,16}... | collective-permute-start | bytes 393224 | tf_op jit(solution)/shard_map/ppermute | solution.py:13
  12.6 4.7 %collective-permute-start.5 = (bf16[256,256]{1,0:T(8,128)(2,1)S(1)}, bf16[256,256]{1,0:T(8,128)(2,1)S(1)}, u32[]{:S(2)}, u32[]{:S(2)}) collective-permute-start(bf16[256,256]{1,0:T(8,128)(2,1)S(1)} %constant_dynamic-update-slice_fusion), channel_id=1, source_target_pairs={{0,6},{1,7},{2,8},{3,9},{4,10},{5,11},{6,12},{7,13},{8,14},{9,15},... | collective-permute-start | bytes 393224 | tf_op jit(solution)/shard_map/ppermute | solution.py:13
  17.3 3.9 %collective-permute-start.4 = (bf16[256,256]{1,0:T(8,128)(2,1)S(1)}, bf16[256,256]{1,0:T(8,128)(2,1)S(1)}, u32[]{:S(2)}, u32[]{:S(2)}) collective-permute-start(bf16[256,256]{1,0:T(8,128)(2,1)S(1)} %constant_dynamic-update-slice_fusion), channel_id=1, source_target_pairs={{0,5},{1,6},{2,7},{3,8},{4,9},{5,10},{6,11},{7,12},{8,13},{9,14},{... | collective-permute-start | bytes 393224 | tf_op jit(solution)/shard_map/ppermute | solution.py:13
  21.3 4.8 %collective-permute-start.3 = (bf16[256,256]{1,0:T(8,128)(2,1)S(1)}, bf16[256,256]{1,0:T(8,128)(2,1)S(1)}, u32[]{:S(2)}, u32[]{:S(2)}) collective-permute-start(bf16[256,256]{1,0:T(8,128)(2,1)S(1)} %constant_dynamic-update-slice_fusion), channel_id=1, source_target_pairs={{0,4},{1,5},{2,6},{3,7},{4,8},{5,9},{6,10},{7,11},{8,12},{9,13},{1... | collective-permute-start | bytes 393224 | tf_op jit(solution)/shard_map/ppermute | solution.py:13
  26.1 1.9 %collective-permute-start = (bf16[256,256]{1,0:T(8,128)(2,1)S(1)}, bf16[256,256]{1,0:T(8,128)(2,1)S(1)}, u32[]{:S(2)}, u32[]{:S(2)}) collective-permute-start(bf16[256,256]{1,0:T(8,128)(2,1)S(1)} %constant_dynamic-update-slice_fusion), channel_id=1, source_target_pairs={{0,1},{1,2},{2,3},{3,4},{4,5},{5,6},{6,7},{7,8},{8,9},{9,10},{10,1... | collective-permute-start | bytes 393224 | tf_op jit(solution)/shard_map/ppermute | solution.py:13
  28.0 0.0 all-gather.2.cloned.1.call-update
  28.0 0.0 reduce-scatter.2.cloned.1.call-start
  28.1 0.1 add_bitcast_fusion
  28.2 0.7 copy.43
  29.0 0.1 reduce.1
  29.1 0.7 sub.31
  29.8 0.1 select_reduce_fusion
  29.8 0.6 compare_and_fusion
  30.4 1.1 copy.75
  31.5 0.8 collective-permute-done
  32.4 3.4 %collective-permute-start.1 = (bf16[256,256]{1,0:T(8,128)(2,1)S(1)}, bf16[256,256]{1,0:T(8,128)(2,1)S(1)}, u32[]{:S(2)}, u32[]{:S(2)}) collective-permute-start(bf16[256,256]{1,0:T(8,128)(2,1)S(1)} %constant_dynamic-update-slice_fusion), channel_id=1, source_target_pairs={{0,2},{1,3},{2,4},{3,5},{4,6},{5,7},{6,8},{7,9},{8,10},{9,11},{10,... | collective-permute-start | bytes 393224 | tf_op jit(solution)/shard_map/ppermute | solution.py:13
  35.8 4.6 %collective-permute-done.1 = bf16[256,256]{1,0:T(8,128)(2,1)S(1)} collective-permute-done((bf16[256,256]{1,0:T(8,128)(2,1)S(1)}, bf16[256,256]{1,0:T(8,128)(2,1)S(1)}, u32[]{:S(2)}, u32[]{:S(2)}) %collective-permute-start.1) | collective-permute-done | bytes 131104 | tf_op jit(solution)/shard_map/ppermute | solution.py:13
  40.4 2.9 %collective-permute-start.2 = (bf16[256,256]{1,0:T(8,128)(2,1)S(1)}, bf16[256,256]{1,0:T(8,128)(2,1)S(1)}, u32[]{:S(2)}, u32[]{:S(2)}) collective-permute-start(bf16[256,256]{1,0:T(8,128)(2,1)S(1)} %constant_dynamic-update-slice_fusion), channel_id=1, source_target_pairs={{0,3},{1,4},{2,5},{3,6},{4,7},{5,8},{6,9},{7,10},{8,11},{9,12},{10... | collective-permute-start | bytes 393224 | tf_op jit(solution)/shard_map/ppermute | solution.py:13
  43.4 2.5 %collective-permute-done.2 = bf16[256,256]{1,0:T(8,128)(2,1)S(1)} collective-permute-done((bf16[256,256]{1,0:T(8,128)(2,1)S(1)}, bf16[256,256]{1,0:T(8,128)(2,1)S(1)}, u32[]{:S(2)}, u32[]{:S(2)}) %collective-permute-start.2) | collective-permute-done | bytes 131104 | tf_op jit(solution)/shard_map/ppermute | solution.py:13
  45.9 0.0 collective-permute-done.3
  45.9 0.0 collective-permute-done.4
  45.9 0.0 collective-permute-done.5
  46.0 0.0 collective-permute-done.6
  46.0 0.3 fusion.26
  46.3 4.8 %fusion.28 = (f32[4,256]{1,0:T(4,128)S(1)}, f32[4,256,2048]{1,2,0:T(8,128)}) fusion(pred[256,2048]{0,1:T(8,128)(4,1)S(1)} %compare_and_fusion, bf16[2048,128,1]{1,0,2:T(8,128)(2,1)S(1)} %bitcast.79, bf16[256,4,128]{0,2,1:T(8,128)(2,1)S(1)} %bitcast.86), kind=kOutput, calls=%fused_computation.68 | convolution fusion | flops 545261568 | bytes 9703424 | tf_op jit(solution)/shard_map/sub | solution.py:48
  51.1 6.0 %fusion.5 = bf16[4,256,2048]{1,2,0:T(8,128)(2,1)} fusion(f32[4,256,2048]{1,2,0:T(8,128)} %get-tuple-element.28, f32[4,256]{1,0:T(4,128)S(1)} %get-tuple-element.27), kind=kLoop, calls=%fused_computation.24 | loop fusion | flops 4194304 | bytes 12587008 | tf_op jit(solution)/shard_map/convert_element_type | solution.py:50
  57.1 18.4 %all-gather.2.cloned.1.call-done = bf16[4096,256]{1,0:T(8,128)(2,1)} async-done(((bf16[512,256]{1,0:T(8,128)(2,1)}), bf16[4096,256]{1,0:T(8,128)(2,1)}) %all-gather.2.cloned.1.call-update) | async-done | bytes 2097168 | tf_op jit(solution)/shard_map/all_gather | solution.py:67
  75.6 0.0 copy-start
  75.6 4.2 %convolution_convert_fusion = bf16[512,256]{1,0:T(8,128)(2,1)S(1)} fusion(bf16[512,4096]{1,0:T(8,128)(2,1)} %param.9, bf16[4096,256]{1,0:T(8,128)(2,1)} %all-gather.2.cloned.1.call-done), kind=kOutput, calls=%fused_computation.28 | convolution fusion | flops 1073872896 | bytes 6553600 | tf_op jit(solution)/shard_map/dot_general | solution.py:65
  79.8 0.0 copy-start.1
  79.9 0.0 copy-done
  79.9 0.8 fusion.8
  80.7 1.4 copy-done.1
  82.0 3.3 %convolution_bitcast_fusion = f32[4096,256]{0,1:T(8,128)} fusion(bf16[256,512]{0,1:T(8,128)(2,1)S(1)} %bitcast.83, bf16[512,4096]{1,0:T(8,128)(2,1)S(1)} %copy-done.1), kind=kOutput, calls=%fused_computation.5 | convolution fusion | flops 1073741824 | bytes 8650752 | tf_op jit(solution)/shard_map/dot_general | solution.py:57
  85.3 0.0 reduce-scatter.2.cloned.1.call-update
  85.3 3.6 %convolution_bitcast_fusion.1 = f32[2048,128]{0,1:T(8,128)S(1)} fusion(bf16[4,256,2048]{1,2,0:T(8,128)(2,1)} %fusion.5, bf16[4,128,256]{2,1,0:T(8,128)(2,1)S(1)} %bitcast.84), kind=kOutput, calls=%fused_computation.25 | convolution fusion | flops 536870912 | bytes 5505024 | tf_op jit(solution)/shard_map/gtk,gdt->kd/dot_general | solution.py:84
  89.0 4.3 %multiply_convert_fusion = bf16[4,256,2048]{1,2,0:T(8,128)(2,1)S(1)} fusion(bf16[2048,128,1]{1,0,2:T(8,128)(2,1)S(1)} %bitcast.82, bf16[4,128,256]{2,1,0:T(8,128)(2,1)S(1)} %bitcast.85, f32[4,256]{1,0:T(4,128)S(1)} %get-tuple-element.29, f32[4,256,2048]{1,2,0:T(8,128)} %get-tuple-element.28, f32[4,256]{1,0:T(4,128)S(1)} %get-tuple-element.27), kind=kOutput, calls=%fused_computation.2 | convolution fusion | flops 547356672 | bytes 13377536 | tf_op jit(solution)/shard_map/gdt,kd->gtk/dot_general | solution.py:74
  93.3 1.5 convolution_bitcast_fusion.2
  94.8 1.1 fusion.18
  95.9 1.9 %collective-permute-start.7 = (f32[256,256]{0,1:T(8,128)S(1)}, f32[256,256]{0,1:T(8,128)S(1)}, u32[]{:S(2)}, u32[]{:S(2)}) collective-permute-start(f32[256,256]{0,1:T(8,128)S(1)} %get-tuple-element.16), channel_id=1, source_target_pairs={{1,0},{2,1},{3,2},{4,3},{5,4},{6,5},{7,6},{8,7},{9,8},{10,9},{11,1... | collective-permute-start | bytes 786440 | tf_op jit(solution)/shard_map/ppermute | solution.py:13
  97.8 1.9 %collective-permute-start.8 = (f32[256,256]{0,1:T(8,128)S(1)}, f32[256,256]{0,1:T(8,128)S(1)}, u32[]{:S(2)}, u32[]{:S(2)}) collective-permute-start(f32[256,256]{0,1:T(8,128)S(1)} %get-tuple-element.17), channel_id=1, source_target_pairs={{2,0},{3,1},{4,2},{5,3},{6,4},{7,5},{8,6},{9,7},{10,8},{11,9},{12,... | collective-permute-start | bytes 786440 | tf_op jit(solution)/shard_map/ppermute | solution.py:13
  99.7 1.3 collective-permute-start.9
  101.0 1.3 collective-permute-start.10
  102.3 1.3 collective-permute-start.11
  103.6 0.0 collective-permute-done.7
  103.7 1.3 collective-permute-start.13
  105.0 5.1 %collective-permute-done.8 = f32[256,256]{0,1:T(8,128)S(1)} collective-permute-done((f32[256,256]{0,1:T(8,128)S(1)}, f32[256,256]{0,1:T(8,128)S(1)}, u32[]{:S(2)}, u32[]{:S(2)}) %collective-permute-start.8) | collective-permute-done | bytes 262176 | tf_op jit(solution)/shard_map/ppermute | solution.py:13
  110.0 1.3 collective-permute-start.12
  111.3 0.8 convolution_convert_fusion.1
  112.1 0.8 copy.55
  112.9 0.8 collective-permute-done.9
  113.7 8.1 %collective-permute-done.10 = f32[256,256]{0,1:T(8,128)} collective-permute-done((f32[256,256]{0,1:T(8,128)}, f32[256,256]{0,1:T(8,128)}, u32[]{:S(2)}, u32[]{:S(2)}) %collective-permute-start.10) | collective-permute-done | bytes 262176 | tf_op jit(solution)/shard_map/ppermute | solution.py:13
  121.8 2.3 %collective-permute-done.11 = f32[256,256]{0,1:T(8,128)} collective-permute-done((f32[256,256]{0,1:T(8,128)}, f32[256,256]{0,1:T(8,128)}, u32[]{:S(2)}, u32[]{:S(2)}) %collective-permute-start.11) | collective-permute-done | bytes 262176 | tf_op jit(solution)/shard_map/ppermute | solution.py:13
  124.1 11.9 %collective-permute-done.13 = f32[256,256]{0,1:T(8,128)} collective-permute-done((f32[256,256]{0,1:T(8,128)}, f32[256,256]{0,1:T(8,128)}, u32[]{:S(2)}, u32[]{:S(2)}) %collective-permute-start.13) | collective-permute-done | bytes 262176 | tf_op jit(solution)/shard_map/ppermute | solution.py:13
  135.9 6.0 %collective-permute-done.12 = f32[256,256]{0,1:T(8,128)} collective-permute-done((f32[256,256]{0,1:T(8,128)}, f32[256,256]{0,1:T(8,128)}, u32[]{:S(2)}, u32[]{:S(2)}) %collective-permute-start.12) | collective-permute-done | bytes 262176 | tf_op jit(solution)/shard_map/ppermute | solution.py:13
  142.0 1.4 fusion.23
  143.4 0.7 copy.57
  144.1 0.7 copy.56
  144.8 0.0 reduce-scatter.2.cloned.1.call-done
  144.8 1.1 convert_element_type.29
  145.9 0.8 copy.54
  (13 shorter events, 0.1 us)
Async XLA Ops:
  7.2 68.4 %all-gather.2.cloned.1.call-start = ((), (), s32[]{:S(2)}) async-start(), calls=%async_computation.2 | async-start | bytes 2359296 | tf_op jit(solution)/shard_map/all_gather | solution.py:67
  8.9 37.0 %collective-permute-start.6 = (bf16[256,256]{1,0:T(8,128)(2,1)S(1)}, bf16[256,256]{1,0:T(8,128)(2,1)S(1)}, u32[]{:S(2)}, u32[]{:S(2)}) collective-permute-start(bf16[256,256]{1,0:T(8,128)(2,1)S(1)} %constant_dynamic-update-slice_fusion), channel_id=1, source_target_pairs={{0,7},{1,8},{2,9},{3,10},{4,11},{5,12},{6,13},{7,14},{8,15},{9,16}... | collective-permute-start | bytes 393224 | tf_op jit(solution)/shard_map/ppermute | solution.py:13
  12.6 33.3 %collective-permute-start.5 = (bf16[256,256]{1,0:T(8,128)(2,1)S(1)}, bf16[256,256]{1,0:T(8,128)(2,1)S(1)}, u32[]{:S(2)}, u32[]{:S(2)}) collective-permute-start(bf16[256,256]{1,0:T(8,128)(2,1)S(1)} %constant_dynamic-update-slice_fusion), channel_id=1, source_target_pairs={{0,6},{1,7},{2,8},{3,9},{4,10},{5,11},{6,12},{7,13},{8,14},{9,15},... | collective-permute-start | bytes 393224 | tf_op jit(solution)/shard_map/ppermute | solution.py:13
  17.3 28.6 %collective-permute-start.4 = (bf16[256,256]{1,0:T(8,128)(2,1)S(1)}, bf16[256,256]{1,0:T(8,128)(2,1)S(1)}, u32[]{:S(2)}, u32[]{:S(2)}) collective-permute-start(bf16[256,256]{1,0:T(8,128)(2,1)S(1)} %constant_dynamic-update-slice_fusion), channel_id=1, source_target_pairs={{0,5},{1,6},{2,7},{3,8},{4,9},{5,10},{6,11},{7,12},{8,13},{9,14},{... | collective-permute-start | bytes 393224 | tf_op jit(solution)/shard_map/ppermute | solution.py:13
  21.3 24.6 %collective-permute-start.3 = (bf16[256,256]{1,0:T(8,128)(2,1)S(1)}, bf16[256,256]{1,0:T(8,128)(2,1)S(1)}, u32[]{:S(2)}, u32[]{:S(2)}) collective-permute-start(bf16[256,256]{1,0:T(8,128)(2,1)S(1)} %constant_dynamic-update-slice_fusion), channel_id=1, source_target_pairs={{0,4},{1,5},{2,6},{3,7},{4,8},{5,9},{6,10},{7,11},{8,12},{9,13},{1... | collective-permute-start | bytes 393224 | tf_op jit(solution)/shard_map/ppermute | solution.py:13
  26.1 6.3 %collective-permute-start = (bf16[256,256]{1,0:T(8,128)(2,1)S(1)}, bf16[256,256]{1,0:T(8,128)(2,1)S(1)}, u32[]{:S(2)}, u32[]{:S(2)}) collective-permute-start(bf16[256,256]{1,0:T(8,128)(2,1)S(1)} %constant_dynamic-update-slice_fusion), channel_id=1, source_target_pairs={{0,1},{1,2},{2,3},{3,4},{4,5},{5,6},{6,7},{7,8},{8,9},{9,10},{10,1... | collective-permute-start | bytes 393224 | tf_op jit(solution)/shard_map/ppermute | solution.py:13
  28.0 116.8 %reduce-scatter.2.cloned.1.call-start = ((), (), s32[]{:S(2)}) async-start(), calls=%async_computation.1 | async-start | bytes 4718592 | tf_op jit(solution)/shard_map/reduce_scatter | solution.py:56
  32.4 8.1 %collective-permute-start.1 = (bf16[256,256]{1,0:T(8,128)(2,1)S(1)}, bf16[256,256]{1,0:T(8,128)(2,1)S(1)}, u32[]{:S(2)}, u32[]{:S(2)}) collective-permute-start(bf16[256,256]{1,0:T(8,128)(2,1)S(1)} %constant_dynamic-update-slice_fusion), channel_id=1, source_target_pairs={{0,2},{1,3},{2,4},{3,5},{4,6},{5,7},{6,8},{7,9},{8,10},{9,11},{10,... | collective-permute-start | bytes 393224 | tf_op jit(solution)/shard_map/ppermute | solution.py:13
  40.4 5.4 %collective-permute-start.2 = (bf16[256,256]{1,0:T(8,128)(2,1)S(1)}, bf16[256,256]{1,0:T(8,128)(2,1)S(1)}, u32[]{:S(2)}, u32[]{:S(2)}) collective-permute-start(bf16[256,256]{1,0:T(8,128)(2,1)S(1)} %constant_dynamic-update-slice_fusion), channel_id=1, source_target_pairs={{0,3},{1,4},{2,5},{3,6},{4,7},{5,8},{6,9},{7,10},{8,11},{9,12},{10... | collective-permute-start | bytes 393224 | tf_op jit(solution)/shard_map/ppermute | solution.py:13
  75.6 4.3 %copy-start = (bf16[4,256,2048]{1,2,0:T(8,128)(2,1)S(1)}, bf16[4,256,2048]{1,2,0:T(8,128)(2,1)}, u32[]{:S(2)}) copy-start(bf16[4,256,2048]{1,2,0:T(8,128)(2,1)} %fusion.5) | copy-start | bytes 12582916
  79.8 2.2 %copy-start.1 = (bf16[512,4096]{1,0:T(8,128)(2,1)S(1)}, bf16[512,4096]{1,0:T(8,128)(2,1)}, u32[]{:S(2)}) copy-start(bf16[512,4096]{1,0:T(8,128)(2,1)} %param.9) | copy-start | bytes 12582916
  95.9 7.7 %collective-permute-start.7 = (f32[256,256]{0,1:T(8,128)S(1)}, f32[256,256]{0,1:T(8,128)S(1)}, u32[]{:S(2)}, u32[]{:S(2)}) collective-permute-start(f32[256,256]{0,1:T(8,128)S(1)} %get-tuple-element.16), channel_id=1, source_target_pairs={{1,0},{2,1},{3,2},{4,3},{5,4},{6,5},{7,6},{8,7},{9,8},{10,9},{11,1... | collective-permute-start | bytes 786440 | tf_op jit(solution)/shard_map/ppermute | solution.py:13
  97.8 12.2 %collective-permute-start.8 = (f32[256,256]{0,1:T(8,128)S(1)}, f32[256,256]{0,1:T(8,128)S(1)}, u32[]{:S(2)}, u32[]{:S(2)}) collective-permute-start(f32[256,256]{0,1:T(8,128)S(1)} %get-tuple-element.17), channel_id=1, source_target_pairs={{2,0},{3,1},{4,2},{5,3},{6,4},{7,5},{8,6},{9,7},{10,8},{11,9},{12,... | collective-permute-start | bytes 786440 | tf_op jit(solution)/shard_map/ppermute | solution.py:13
  99.7 14.0 %collective-permute-start.9 = (f32[256,256]{0,1:T(8,128)}, f32[256,256]{0,1:T(8,128)}, u32[]{:S(2)}, u32[]{:S(2)}) collective-permute-start(f32[256,256]{0,1:T(8,128)} %get-tuple-element.18), channel_id=1, source_target_pairs={{3,0},{4,1},{5,2},{6,3},{7,4},{8,5},{9,6},{10,7},{11,8},{12,9},{13... | collective-permute-start | bytes 786440 | tf_op jit(solution)/shard_map/ppermute | solution.py:13
  101.0 20.8 %collective-permute-start.10 = (f32[256,256]{0,1:T(8,128)}, f32[256,256]{0,1:T(8,128)}, u32[]{:S(2)}, u32[]{:S(2)}) collective-permute-start(f32[256,256]{0,1:T(8,128)} %get-tuple-element.19), channel_id=1, source_target_pairs={{4,0},{5,1},{6,2},{7,3},{8,4},{9,5},{10,6},{11,7},{12,8},{13,9},{1... | collective-permute-start | bytes 786440 | tf_op jit(solution)/shard_map/ppermute | solution.py:13
  102.3 21.7 %collective-permute-start.11 = (f32[256,256]{0,1:T(8,128)}, f32[256,256]{0,1:T(8,128)}, u32[]{:S(2)}, u32[]{:S(2)}) collective-permute-start(f32[256,256]{0,1:T(8,128)} %get-tuple-element.20), channel_id=1, source_target_pairs={{5,0},{6,1},{7,2},{8,3},{9,4},{10,5},{11,6},{12,7},{13,8},{14,9},{... | collective-permute-start | bytes 786440 | tf_op jit(solution)/shard_map/ppermute | solution.py:13
  103.7 32.3 %collective-permute-start.13 = (f32[256,256]{0,1:T(8,128)}, f32[256,256]{0,1:T(8,128)}, u32[]{:S(2)}, u32[]{:S(2)}) collective-permute-start(f32[256,256]{0,1:T(8,128)} %get-tuple-element.21), channel_id=1, source_target_pairs={{7,0},{8,1},{9,2},{10,3},{11,4},{12,5},{13,6},{14,7},{15,8},{16,9}... | collective-permute-start | bytes 786440 | tf_op jit(solution)/shard_map/ppermute | solution.py:13
  110.0 32.0 %collective-permute-start.12 = (f32[256,256]{0,1:T(8,128)}, f32[256,256]{0,1:T(8,128)}, u32[]{:S(2)}, u32[]{:S(2)}) collective-permute-start(f32[256,256]{0,1:T(8,128)} %get-tuple-element.22), channel_id=1, source_target_pairs={{6,0},{7,1},{8,2},{9,3},{10,4},{11,5},{12,6},{13,7},{14,8},{15,9},... | collective-permute-start | bytes 786440 | tf_op jit(solution)/shard_map/ppermute | solution.py:13
Sparse Core Ops, SparseCore 0:
  28.2 47.3 all-gather.1
  85.5 55.6 reduce-scatter.1
where the time goes:
time: 154 us
  waiting for transfers between devices  60.6 us (39%)
  starting transfers between devices  35.7 us (23%)
  matrix products  23.4 us (15%)
  between operations  14.4 us (9%)
  other arithmetic  11.1 us (7%)
  local copies, waits for them, and re-layouts  8.43 us (5%)
    ppermute x14, waiting for transfers between devices, passed_along(): lax.ppermute(value, axis, [(source, source + steps) for source in range(f...  42.1 us
    ppermute x14, starting transfers between devices, passed_along(): lax.ppermute(value, axis, [(source, source + steps) for source in range(f...  35.6 us
    all_gather x1, waiting for transfers between devices, per_device(): lax.all_gather(out_grad, 'heads', axis=0, tiled=True)  18.4 us
    convert_element_type x1, other arithmetic, per_device(): probs = weights.astype(jnp.bfloat16)  6.04 us
    unnamed x17, local copies, waits for them, and re-layouts  5.47 us
    sub x1, matrix products, per_device(): expons = jnp.exp(scores - largest)  4.84 us
    dot_general x1, matrix products, per_device(): jnp.einsum('gdt,kd->gtk', grad_heads, flat_values, preferred_element_type...  4.34 us
    dot_general x1, matrix products, per_device(): jnp.dot(columns, lax.all_gather(out_grad, 'heads', axis=0, tiled=True), p...  4.25 us
  transfers between devices with their start and end apart: 16, of which 10 were waited for; matrix products, arithmetic and copies ran while one was open for 19% of the time, Pallas kernels for 0%

commit v1 on v0

--- a/solution.py
+++ b/solution.py
@@ -64,7 +64,9 @@
     columns = out_weight
     grad_attn = jnp.dot(
         columns,
-        lax.all_gather(out_grad, "heads", axis=0, tiled=True),
+        jnp.concatenate(
+            lax.all_to_all(jnp.stack([out_grad] * lax.axis_size("heads")), "heads", 0, 0), axis=0
+        ),
         preferred_element_type=jnp.float32,
     ).astype(jnp.bfloat16)
     grad_heads = grad_attn.reshape(group_size, head_dim, tok_rows)

time: 154 us -> 174 us (1.13)
  the two profiles are of different devices: /device:TPU:10 before, /device:TPU:66 now
where the time goes in v1:
time: 174 us; the launch traced here: 173 us
  waiting for transfers between devices  65.2 us (37%)
  starting transfers between devices  49.8 us (29%)
  matrix products  23.6 us (14%)
  between operations  14.4 us (8%)
  other arithmetic  11.2 us (6%)
  local copies, waits for them, and re-layouts  9.34 us (5%)
    ppermute x14, waiting for transfers between devices, passed_along(): lax.ppermute(value, axis, [(source, source + steps) for source in range(f...  43.6 us
    ppermute x14, starting transfers between devices, passed_along(): lax.ppermute(value, axis, [(source, source + steps) for source in range(f...  42.6 us
    all_to_all x1, waiting for transfers between devices, per_device(): lax.all_to_all(jnp.stack([out_grad] * lax.axis_size('heads')), 'heads', 0...  21.6 us
    all_to_all x1, starting transfers between devices, per_device(): lax.all_to_all(jnp.stack([out_grad] * lax.axis_size('heads')), 'heads', 0...  7.1 us
    convert_element_type x1, other arithmetic, per_device(): probs = weights.astype(jnp.bfloat16)  6.01 us
    sub x1, matrix products, per_device(): expons = jnp.exp(scores - largest)  5.74 us
    unnamed x25, local copies, waits for them, and re-layouts  5.54 us
    dot_general x1, matrix products, per_device(): jnp.einsum('gdt,kd->gtk', grad_heads, flat_values, preferred_element_type...  4.37 us
  transfers between devices with their start and end apart: 16, of which 8 were waited for; matrix products, arithmetic and copies ran while one was open for 18% of the time, Pallas kernels for 0%

profile of v1, /device:TPU:66, one launch (start us, length us, event | category | flops | bytes accessed | tf_op | source)
XLA Modules:
  0.0 173.5 jit_solution(7016793121162407497)
XLA Ops:
  7.2 0.9 constant_dynamic-update-slice_fusion.1
  8.1 0.9 constant_dynamic-update-slice_fusion
  8.9 3.7 %collective-permute-start.6 = (bf16[256,256]{1,0:T(8,128)(2,1)S(1)}, bf16[256,256]{1,0:T(8,128)(2,1)S(1)}, u32[]{:S(2)}, u32[]{:S(2)}) collective-permute-start(bf16[256,256]{1,0:T(8,128)(2,1)S(1)} %constant_dynamic-update-slice_fusion), channel_id=1, source_target_pairs={{0,7},{1,8},{2,9},{3,10},{4,11},{5,12},{6,13},{7,14},{8,15},{9,16}... | collective-permute-start | bytes 393224 | tf_op jit(solution)/shard_map/ppermute | solution.py:13
  12.6 4.7 %collective-permute-start.5 = (bf16[256,256]{1,0:T(8,128)(2,1)S(1)}, bf16[256,256]{1,0:T(8,128)(2,1)S(1)}, u32[]{:S(2)}, u32[]{:S(2)}) collective-permute-start(bf16[256,256]{1,0:T(8,128)(2,1)S(1)} %constant_dynamic-update-slice_fusion), channel_id=1, source_target_pairs={{0,6},{1,7},{2,8},{3,9},{4,10},{5,11},{6,12},{7,13},{8,14},{9,15},... | collective-permute-start | bytes 393224 | tf_op jit(solution)/shard_map/ppermute | solution.py:13
  17.3 3.9 %collective-permute-start.4 = (bf16[256,256]{1,0:T(8,128)(2,1)S(1)}, bf16[256,256]{1,0:T(8,128)(2,1)S(1)}, u32[]{:S(2)}, u32[]{:S(2)}) collective-permute-start(bf16[256,256]{1,0:T(8,128)(2,1)S(1)} %constant_dynamic-update-slice_fusion), channel_id=1, source_target_pairs={{0,5},{1,6},{2,7},{3,8},{4,9},{5,10},{6,11},{7,12},{8,13},{9,14},{... | collective-permute-start | bytes 393224 | tf_op jit(solution)/shard_map/ppermute | solution.py:13
  21.3 6.0 %collective-permute-start.3 = (bf16[256,256]{1,0:T(8,128)(2,1)S(1)}, bf16[256,256]{1,0:T(8,128)(2,1)S(1)}, u32[]{:S(2)}, u32[]{:S(2)}) collective-permute-start(bf16[256,256]{1,0:T(8,128)(2,1)S(1)} %constant_dynamic-update-slice_fusion), channel_id=1, source_target_pairs={{0,4},{1,5},{2,6},{3,7},{4,8},{5,9},{6,10},{7,11},{8,12},{9,13},{1... | collective-permute-start | bytes 393224 | tf_op jit(solution)/shard_map/ppermute | solution.py:13
  27.3 1.9 %collective-permute-start = (bf16[256,256]{1,0:T(8,128)(2,1)S(1)}, bf16[256,256]{1,0:T(8,128)(2,1)S(1)}, u32[]{:S(2)}, u32[]{:S(2)}) collective-permute-start(bf16[256,256]{1,0:T(8,128)(2,1)S(1)} %constant_dynamic-update-slice_fusion), channel_id=1, source_target_pairs={{0,1},{1,2},{2,3},{3,4},{4,5},{5,6},{6,7},{7,8},{8,9},{9,10},{10,1... | collective-permute-start | bytes 393224 | tf_op jit(solution)/shard_map/ppermute | solution.py:13
  29.2 2.4 %stack.2 = bf16[8,512,256]{2,1,0:T(8,128)(2,1)} broadcast(bf16[512,256]{1,0:T(8,128)(2,1)} %param.10), dimensions={1,2} | broadcast | bytes 2359296 | tf_op jit(solution)/shard_map/stack | solution.py:68
  31.7 7.1 %all-to-all-start = ((bf16[8,512,256]{2,1,0:T(8,128)(2,1)}), bf16[8,512,256]{2,1,0:T(8,128)(2,1)S(1)}, u32[]{:S(2)}, u32[]{:S(2)}) async-start(bf16[8,512,256]{2,1,0:T(8,128)(2,1)} %stack.2), calls=%async_computation.1 | async-start | bytes 4194304 | tf_op jit(solution)/shard_map/all_to_all | solution.py:68
  38.8 0.0 reduce-scatter.2.cloned.1.call-start
  38.9 0.1 add_bitcast_fusion
  39.0 0.0 copy-done.5
  39.0 0.1 copy.43
  39.1 0.1 reduce.1
  39.2 0.1 select_reduce_fusion
  39.3 1.3 compare_and_fusion
  40.6 0.1 copy.75
  40.7 0.0 copy-start.2
  40.7 0.0 collective-permute-done
  40.8 3.4 %collective-permute-start.1 = (bf16[256,256]{1,0:T(8,128)(2,1)S(1)}, bf16[256,256]{1,0:T(8,128)(2,1)S(1)}, u32[]{:S(2)}, u32[]{:S(2)}) collective-permute-start(bf16[256,256]{1,0:T(8,128)(2,1)S(1)} %constant_dynamic-update-slice_fusion), channel_id=1, source_target_pairs={{0,2},{1,3},{2,4},{3,5},{4,6},{5,7},{6,8},{7,9},{8,10},{9,11},{10,... | collective-permute-start | bytes 393224 | tf_op jit(solution)/shard_map/ppermute | solution.py:13
  44.2 4.5 %collective-permute-done.1 = bf16[256,256]{1,0:T(8,128)(2,1)S(1)} collective-permute-done((bf16[256,256]{1,0:T(8,128)(2,1)S(1)}, bf16[256,256]{1,0:T(8,128)(2,1)S(1)}, u32[]{:S(2)}, u32[]{:S(2)}) %collective-permute-start.1) | collective-permute-done | bytes 131104 | tf_op jit(solution)/shard_map/ppermute | solution.py:13
  48.7 3.5 %collective-permute-start.2 = (bf16[256,256]{1,0:T(8,128)(2,1)S(1)}, bf16[256,256]{1,0:T(8,128)(2,1)S(1)}, u32[]{:S(2)}, u32[]{:S(2)}) collective-permute-start(bf16[256,256]{1,0:T(8,128)(2,1)S(1)} %constant_dynamic-update-slice_fusion), channel_id=1, source_target_pairs={{0,3},{1,4},{2,5},{3,6},{4,7},{5,8},{6,9},{7,10},{8,11},{9,12},{10... | collective-permute-start | bytes 393224 | tf_op jit(solution)/shard_map/ppermute | solution.py:13
  52.2 5.5 %collective-permute-done.2 = bf16[256,256]{1,0:T(8,128)(2,1)S(1)} collective-permute-done((bf16[256,256]{1,0:T(8,128)(2,1)S(1)}, bf16[256,256]{1,0:T(8,128)(2,1)S(1)}, u32[]{:S(2)}, u32[]{:S(2)}) %collective-permute-start.2) | collective-permute-done | bytes 131104 | tf_op jit(solution)/shard_map/ppermute | solution.py:13
  57.7 0.0 collective-permute-done.3
  57.7 0.0 collective-permute-done.4
  57.8 0.0 collective-permute-done.5
  57.8 0.0 collective-permute-done.6
  57.8 0.3 fusion.26
  58.1 5.7 %fusion.28 = (f32[4,256]{1,0:T(4,128)S(1)}, f32[4,256,2048]{1,2,0:T(8,128)}) fusion(pred[256,2048]{0,1:T(8,128)(4,1)} %compare_and_fusion, bf16[2048,128,1]{1,0,2:T(8,128)(2,1)S(1)} %bitcast.81, bf16[256,4,128]{0,2,1:T(8,128)(2,1)S(1)} %bitcast.88), kind=kOutput, calls=%fused_computation.68 | convolution fusion | flops 545261568 | bytes 9703424 | tf_op jit(solution)/shard_map/sub | solution.py:48
  63.8 0.0 copy-done.2
  63.9 6.0 %fusion.5 = bf16[4,256,2048]{1,2,0:T(8,128)(2,1)} fusion(f32[4,256,2048]{1,2,0:T(8,128)} %get-tuple-element.28, f32[4,256]{1,0:T(4,128)S(1)} %get-tuple-element.27), kind=kLoop, calls=%fused_computation.24 | loop fusion | flops 4194304 | bytes 12587008 | tf_op jit(solution)/shard_map/convert_element_type | solution.py:50
  69.9 21.6 %all-to-all-done = bf16[8,512,256]{2,1,0:T(8,128)(2,1)S(1)} async-done(((bf16[8,512,256]{2,1,0:T(8,128)(2,1)}), bf16[8,512,256]{2,1,0:T(8,128)(2,1)S(1)}, u32[]{:S(2)}, u32[]{:S(2)}) %all-to-all-start) | async-done | bytes 2097184 | tf_op jit(solution)/shard_map/all_to_all | solution.py:68
  91.4 3.6 %convolution_convert_fusion = bf16[512,256]{1,0:T(8,128)(2,1)S(1)} fusion(bf16[512,4096]{1,0:T(8,128)(2,1)} %param.9, bf16[4096,256]{1,0:T(8,128)(2,1)S(1)} %bitcast.80), kind=kOutput, calls=%fused_computation.28 | convolution fusion | flops 1073872896 | bytes 6553600 | tf_op jit(solution)/shard_map/dot_general | solution.py:65
  95.0 0.0 copy-start.1
  95.1 0.8 fusion.8
  95.9 1.4 copy-done.1
  97.2 3.3 %convolution_bitcast_fusion = f32[4096,256]{0,1:T(8,128)} fusion(bf16[256,512]{0,1:T(8,128)(2,1)S(1)} %bitcast.85, bf16[512,4096]{1,0:T(8,128)(2,1)S(1)} %copy-done.1), kind=kOutput, calls=%fused_computation.5 | convolution fusion | flops 1073741824 | bytes 8650752 | tf_op jit(solution)/shard_map/dot_general | solution.py:57
  100.5 0.0 reduce-scatter.2.cloned.1.call-update
  100.5 3.7 %convolution_bitcast_fusion.1 = f32[2048,128]{0,1:T(8,128)S(1)} fusion(bf16[4,256,2048]{1,2,0:T(8,128)(2,1)} %fusion.5, bf16[4,128,256]{2,1,0:T(8,128)(2,1)S(1)} %bitcast.86), kind=kOutput, calls=%fused_computation.25 | convolution fusion | flops 536870912 | bytes 5505024 | tf_op jit(solution)/shard_map/gtk,gdt->kd/dot_general | solution.py:86
  104.2 0.0 copy-start.3
  104.2 4.4 %multiply_convert_fusion = bf16[4,256,2048]{1,2,0:T(8,128)(2,1)S(1)} fusion(bf16[2048,128,1]{1,0,2:T(8,128)(2,1)S(1)} %bitcast.84, bf16[4,128,256]{2,1,0:T(8,128)(2,1)S(1)} %bitcast.87, f32[4,256]{1,0:T(4,128)S(1)} %get-tuple-element.29, f32[4,256,2048]{1,2,0:T(8,128)} %get-tuple-element.28, f32[4,256]{1,0:T(4,128)S(1)} %get-tuple-element.27), kind=kOutput, calls=%fused_computation.2 | convolution fusion | flops 547356672 | bytes 13377536 | tf_op jit(solution)/shard_map/gdt,kd->gtk/dot_general | solution.py:76
  108.6 1.5 convolution_bitcast_fusion.2
  110.1 1.1 fusion.18
  111.1 1.9 %collective-permute-start.7 = (f32[256,256]{0,1:T(8,128)S(1)}, f32[256,256]{0,1:T(8,128)S(1)}, u32[]{:S(2)}, u32[]{:S(2)}) collective-permute-start(f32[256,256]{0,1:T(8,128)S(1)} %get-tuple-element.16), channel_id=1, source_target_pairs={{1,0},{2,1},{3,2},{4,3},{5,4},{6,5},{7,6},{8,7},{9,8},{10,9},{11,1... | collective-permute-start | bytes 786440 | tf_op jit(solution)/shard_map/ppermute | solution.py:13
  113.1 3.4 %collective-permute-start.8 = (f32[256,256]{0,1:T(8,128)S(1)}, f32[256,256]{0,1:T(8,128)S(1)}, u32[]{:S(2)}, u32[]{:S(2)}) collective-permute-start(f32[256,256]{0,1:T(8,128)S(1)} %get-tuple-element.17), channel_id=1, source_target_pairs={{2,0},{3,1},{4,2},{5,3},{6,4},{7,5},{8,6},{9,7},{10,8},{11,9},{12,... | collective-permute-start | bytes 786440 | tf_op jit(solution)/shard_map/ppermute | solution.py:13
  116.5 1.9 %collective-permute-start.9 = (f32[256,256]{0,1:T(8,128)}, f32[256,256]{0,1:T(8,128)}, u32[]{:S(2)}, u32[]{:S(2)}) collective-permute-start(f32[256,256]{0,1:T(8,128)} %get-tuple-element.18), channel_id=1, source_target_pairs={{3,0},{4,1},{5,2},{6,3},{7,4},{8,5},{9,6},{10,7},{11,8},{12,9},{13... | collective-permute-start | bytes 786440 | tf_op jit(solution)/shard_map/ppermute | solution.py:13
  118.4 2.5 %collective-permute-start.10 = (f32[256,256]{0,1:T(8,128)}, f32[256,256]{0,1:T(8,128)}, u32[]{:S(2)}, u32[]{:S(2)}) collective-permute-start(f32[256,256]{0,1:T(8,128)} %get-tuple-element.19), channel_id=1, source_target_pairs={{4,0},{5,1},{6,2},{7,3},{8,4},{9,5},{10,6},{11,7},{12,8},{13,9},{1... | collective-permute-start | bytes 786440 | tf_op jit(solution)/shard_map/ppermute | solution.py:13
  120.9 1.9 %collective-permute-start.11 = (f32[256,256]{0,1:T(8,128)}, f32[256,256]{0,1:T(8,128)}, u32[]{:S(2)}, u32[]{:S(2)}) collective-permute-start(f32[256,256]{0,1:T(8,128)} %get-tuple-element.20), channel_id=1, source_target_pairs={{5,0},{6,1},{7,2},{8,3},{9,4},{10,5},{11,6},{12,7},{13,8},{14,9},{... | collective-permute-start | bytes 786440 | tf_op jit(solution)/shard_map/ppermute | solution.py:13
  122.9 0.0 collective-permute-done.7
  122.9 1.9 %collective-permute-start.13 = (f32[256,256]{0,1:T(8,128)}, f32[256,256]{0,1:T(8,128)}, u32[]{:S(2)}, u32[]{:S(2)}) collective-permute-start(f32[256,256]{0,1:T(8,128)} %get-tuple-element.21), channel_id=1, source_target_pairs={{7,0},{8,1},{9,2},{10,3},{11,4},{12,5},{13,6},{14,7},{15,8},{16,9}... | collective-permute-start | bytes 786440 | tf_op jit(solution)/shard_map/ppermute | solution.py:13
  124.8 0.9 collective-permute-done.8
  125.7 1.9 %collective-permute-start.12 = (f32[256,256]{0,1:T(8,128)}, f32[256,256]{0,1:T(8,128)}, u32[]{:S(2)}, u32[]{:S(2)}) collective-permute-start(f32[256,256]{0,1:T(8,128)} %get-tuple-element.22), channel_id=1, source_target_pairs={{6,0},{7,1},{8,2},{9,3},{10,4},{11,5},{12,6},{13,7},{14,8},{15,9},... | collective-permute-start | bytes 786440 | tf_op jit(solution)/shard_map/ppermute | solution.py:13
  127.7 0.8 convolution_convert_fusion.1
  128.4 0.8 copy.55
  129.3 0.0 collective-permute-done.9
  129.3 8.8 %collective-permute-done.10 = f32[256,256]{0,1:T(8,128)} collective-permute-done((f32[256,256]{0,1:T(8,128)}, f32[256,256]{0,1:T(8,128)}, u32[]{:S(2)}, u32[]{:S(2)}) %collective-permute-start.10) | collective-permute-done | bytes 262176 | tf_op jit(solution)/shard_map/ppermute | solution.py:13
  138.1 5.1 %collective-permute-done.11 = f32[256,256]{0,1:T(8,128)} collective-permute-done((f32[256,256]{0,1:T(8,128)}, f32[256,256]{0,1:T(8,128)}, u32[]{:S(2)}, u32[]{:S(2)}) %collective-permute-start.11) | collective-permute-done | bytes 262176 | tf_op jit(solution)/shard_map/ppermute | solution.py:13
  143.1 12.1 %collective-permute-done.13 = f32[256,256]{0,1:T(8,128)} collective-permute-done((f32[256,256]{0,1:T(8,128)}, f32[256,256]{0,1:T(8,128)}, u32[]{:S(2)}, u32[]{:S(2)}) %collective-permute-start.13) | collective-permute-done | bytes 262176 | tf_op jit(solution)/shard_map/ppermute | solution.py:13
  155.2 6.6 %collective-permute-done.12 = f32[256,256]{0,1:T(8,128)} collective-permute-done((f32[256,256]{0,1:T(8,128)}, f32[256,256]{0,1:T(8,128)}, u32[]{:S(2)}, u32[]{:S(2)}) %collective-permute-start.12) | collective-permute-done | bytes 262176 | tf_op jit(solution)/shard_map/ppermute | solution.py:13
  161.9 1.4 fusion.23
  163.3 0.7 copy.57
  164.0 0.7 copy.56
  164.7 1.1 convert_element_type.29
  165.8 0.8 copy.54
  (21 shorter events, 0.2 us)
Async XLA Ops:
  7.2 31.8 %copy-start.5 = (s32[16]{0:T(128)S(1)}, s32[16]{0:T(128)}, u32[]{:S(2)}) copy-start(s32[16]{0:T(128)} %param.11) | copy-start | bytes 196
  7.2 33.4 %copy-start.4 = (bf16[256,512]{1,0:T(8,128)(2,1)S(1)}, bf16[256,512]{1,0:T(8,128)(2,1)}, u32[]{:S(2)}) copy-start(bf16[256,512]{1,0:T(8,128)(2,1)} %param.6) | copy-start | bytes 786436
  8.9 48.9 %collective-permute-start.6 = (bf16[256,256]{1,0:T(8,128)(2,1)S(1)}, bf16[256,256]{1,0:T(8,128)(2,1)S(1)}, u32[]{:S(2)}, u32[]{:S(2)}) collective-permute-start(bf16[256,256]{1,0:T(8,128)(2,1)S(1)} %constant_dynamic-update-slice_fusion), channel_id=1, source_target_pairs={{0,7},{1,8},{2,9},{3,10},{4,11},{5,12},{6,13},{7,14},{8,15},{9,16}... | collective-permute-start | bytes 393224 | tf_op jit(solution)/shard_map/ppermute | solution.py:13
  12.6 45.1 %collective-permute-start.5 = (bf16[256,256]{1,0:T(8,128)(2,1)S(1)}, bf16[256,256]{1,0:T(8,128)(2,1)S(1)}, u32[]{:S(2)}, u32[]{:S(2)}) collective-permute-start(bf16[256,256]{1,0:T(8,128)(2,1)S(1)} %constant_dynamic-update-slice_fusion), channel_id=1, source_target_pairs={{0,6},{1,7},{2,8},{3,9},{4,10},{5,11},{6,12},{7,13},{8,14},{9,15},... | collective-permute-start | bytes 393224 | tf_op jit(solution)/shard_map/ppermute | solution.py:13
  17.3 40.4 %collective-permute-start.4 = (bf16[256,256]{1,0:T(8,128)(2,1)S(1)}, bf16[256,256]{1,0:T(8,128)(2,1)S(1)}, u32[]{:S(2)}, u32[]{:S(2)}) collective-permute-start(bf16[256,256]{1,0:T(8,128)(2,1)S(1)} %constant_dynamic-update-slice_fusion), channel_id=1, source_target_pairs={{0,5},{1,6},{2,7},{3,8},{4,9},{5,10},{6,11},{7,12},{8,13},{9,14},{... | collective-permute-start | bytes 393224 | tf_op jit(solution)/shard_map/ppermute | solution.py:13
  21.3 36.5 %collective-permute-start.3 = (bf16[256,256]{1,0:T(8,128)(2,1)S(1)}, bf16[256,256]{1,0:T(8,128)(2,1)S(1)}, u32[]{:S(2)}, u32[]{:S(2)}) collective-permute-start(bf16[256,256]{1,0:T(8,128)(2,1)S(1)} %constant_dynamic-update-slice_fusion), channel_id=1, source_target_pairs={{0,4},{1,5},{2,6},{3,7},{4,8},{5,9},{6,10},{7,11},{8,12},{9,13},{1... | collective-permute-start | bytes 393224 | tf_op jit(solution)/shard_map/ppermute | solution.py:13
  27.3 13.4 %collective-permute-start = (bf16[256,256]{1,0:T(8,128)(2,1)S(1)}, bf16[256,256]{1,0:T(8,128)(2,1)S(1)}, u32[]{:S(2)}, u32[]{:S(2)}) collective-permute-start(bf16[256,256]{1,0:T(8,128)(2,1)S(1)} %constant_dynamic-update-slice_fusion), channel_id=1, source_target_pairs={{0,1},{1,2},{2,3},{3,4},{4,5},{5,6},{6,7},{7,8},{8,9},{9,10},{10,1... | collective-permute-start | bytes 393224 | tf_op jit(solution)/shard_map/ppermute | solution.py:13
  31.7 59.8 %all-to-all-start = ((bf16[8,512,256]{2,1,0:T(8,128)(2,1)}), bf16[8,512,256]{2,1,0:T(8,128)(2,1)S(1)}, u32[]{:S(2)}, u32[]{:S(2)}) async-start(bf16[8,512,256]{2,1,0:T(8,128)(2,1)} %stack.2), calls=%async_computation.1 | async-start | bytes 4194304 | tf_op jit(solution)/shard_map/all_to_all | solution.py:68
  38.8 125.9 %reduce-scatter.2.cloned.1.call-start = ((), (), s32[]{:S(2)}) async-start(), calls=%async_computation.2 | async-start | bytes 4718592 | tf_op jit(solution)/shard_map/reduce_scatter | solution.py:56
  40.7 23.1 %copy-start.2 = (bf16[256,512]{0,1:T(8,128)(2,1)}, bf16[256,512]{0,1:T(8,128)(2,1)S(1)}, u32[]{:S(2)}) copy-start(bf16[256,512]{0,1:T(8,128)(2,1)S(1)} %copy.75) | copy-start | bytes 786436
  40.8 7.9 %collective-permute-start.1 = (bf16[256,256]{1,0:T(8,128)(2,1)S(1)}, bf16[256,256]{1,0:T(8,128)(2,1)S(1)}, u32[]{:S(2)}, u32[]{:S(2)}) collective-permute-start(bf16[256,256]{1,0:T(8,128)(2,1)S(1)} %constant_dynamic-update-slice_fusion), channel_id=1, source_target_pairs={{0,2},{1,3},{2,4},{3,5},{4,6},{5,7},{6,8},{7,9},{8,10},{9,11},{10,... | collective-permute-start | bytes 393224 | tf_op jit(solution)/shard_map/ppermute | solution.py:13
  48.7 9.0 %collective-permute-start.2 = (bf16[256,256]{1,0:T(8,128)(2,1)S(1)}, bf16[256,256]{1,0:T(8,128)(2,1)S(1)}, u32[]{:S(2)}, u32[]{:S(2)}) collective-permute-start(bf16[256,256]{1,0:T(8,128)(2,1)S(1)} %constant_dynamic-update-slice_fusion), channel_id=1, source_target_pairs={{0,3},{1,4},{2,5},{3,6},{4,7},{5,8},{6,9},{7,10},{8,11},{9,12},{10... | collective-permute-start | bytes 393224 | tf_op jit(solution)/shard_map/ppermute | solution.py:13
  91.4 3.6 %copy-start = (bf16[4,256,2048]{1,2,0:T(8,128)(2,1)S(1)}, bf16[4,256,2048]{1,2,0:T(8,128)(2,1)}, u32[]{:S(2)}) copy-start(bf16[4,256,2048]{1,2,0:T(8,128)(2,1)} %fusion.5) | copy-start | bytes 12582916
  95.0 2.2 %copy-start.1 = (bf16[512,4096]{1,0:T(8,128)(2,1)S(1)}, bf16[512,4096]{1,0:T(8,128)(2,1)}, u32[]{:S(2)}) copy-start(bf16[512,4096]{1,0:T(8,128)(2,1)} %param.9) | copy-start | bytes 12582916
  104.2 4.4 %copy-start.3 = (bf16[256,512]{0,1:T(8,128)(2,1)S(1)}, bf16[256,512]{0,1:T(8,128)(2,1)}, u32[]{:S(2)}) copy-start(bf16[256,512]{0,1:T(8,128)(2,1)} %copy-done.2) | copy-start | bytes 786436
  111.1 11.7 %collective-permute-start.7 = (f32[256,256]{0,1:T(8,128)S(1)}, f32[256,256]{0,1:T(8,128)S(1)}, u32[]{:S(2)}, u32[]{:S(2)}) collective-permute-start(f32[256,256]{0,1:T(8,128)S(1)} %get-tuple-element.16), channel_id=1, source_target_pairs={{1,0},{2,1},{3,2},{4,3},{5,4},{6,5},{7,6},{8,7},{9,8},{10,9},{11,1... | collective-permute-start | bytes 786440 | tf_op jit(solution)/shard_map/ppermute | solution.py:13
  113.1 12.7 %collective-permute-start.8 = (f32[256,256]{0,1:T(8,128)S(1)}, f32[256,256]{0,1:T(8,128)S(1)}, u32[]{:S(2)}, u32[]{:S(2)}) collective-permute-start(f32[256,256]{0,1:T(8,128)S(1)} %get-tuple-element.17), channel_id=1, source_target_pairs={{2,0},{3,1},{4,2},{5,3},{6,4},{7,5},{8,6},{9,7},{10,8},{11,9},{12,... | collective-permute-start | bytes 786440 | tf_op jit(solution)/shard_map/ppermute | solution.py:13
  116.5 12.8 %collective-permute-start.9 = (f32[256,256]{0,1:T(8,128)}, f32[256,256]{0,1:T(8,128)}, u32[]{:S(2)}, u32[]{:S(2)}) collective-permute-start(f32[256,256]{0,1:T(8,128)} %get-tuple-element.18), channel_id=1, source_target_pairs={{3,0},{4,1},{5,2},{6,3},{7,4},{8,5},{9,6},{10,7},{11,8},{12,9},{13... | collective-permute-start | bytes 786440 | tf_op jit(solution)/shard_map/ppermute | solution.py:13
  118.4 19.7 %collective-permute-start.10 = (f32[256,256]{0,1:T(8,128)}, f32[256,256]{0,1:T(8,128)}, u32[]{:S(2)}, u32[]{:S(2)}) collective-permute-start(f32[256,256]{0,1:T(8,128)} %get-tuple-element.19), channel_id=1, source_target_pairs={{4,0},{5,1},{6,2},{7,3},{8,4},{9,5},{10,6},{11,7},{12,8},{13,9},{1... | collective-permute-start | bytes 786440 | tf_op jit(solution)/shard_map/ppermute | solution.py:13
  120.9 22.2 %collective-permute-start.11 = (f32[256,256]{0,1:T(8,128)}, f32[256,256]{0,1:T(8,128)}, u32[]{:S(2)}, u32[]{:S(2)}) collective-permute-start(f32[256,256]{0,1:T(8,128)} %get-tuple-element.20), channel_id=1, source_target_pairs={{5,0},{6,1},{7,2},{8,3},{9,4},{10,5},{11,6},{12,7},{13,8},{14,9},{... | collective-permute-start | bytes 786440 | tf_op jit(solution)/shard_map/ppermute | solution.py:13
  122.9 32.3 %collective-permute-start.13 = (f32[256,256]{0,1:T(8,128)}, f32[256,256]{0,1:T(8,128)}, u32[]{:S(2)}, u32[]{:S(2)}) collective-permute-start(f32[256,256]{0,1:T(8,128)} %get-tuple-element.21), channel_id=1, source_target_pairs={{7,0},{8,1},{9,2},{10,3},{11,4},{12,5},{13,6},{14,7},{15,8},{16,9}... | collective-permute-start | bytes 786440 | tf_op jit(solution)/shard_map/ppermute | solution.py:13
  125.7 36.1 %collective-permute-start.12 = (f32[256,256]{0,1:T(8,128)}, f32[256,256]{0,1:T(8,128)}, u32[]{:S(2)}, u32[]{:S(2)}) collective-permute-start(f32[256,256]{0,1:T(8,128)} %get-tuple-element.22), channel_id=1, source_target_pairs={{6,0},{7,1},{8,2},{9,3},{10,4},{11,5},{12,6},{13,7},{14,8},{15,9},... | collective-permute-start | bytes 786440 | tf_op jit(solution)/shard_map/ppermute | solution.py:13
Sparse Core Ops, SparseCore 0:
  100.7 52.6 reduce-scatter.1
